TPU v7x, 256 devices: a whole 4x4x8 slice. The times are simulated.
256 devices in a mesh: seq: 64 (over x, z, core), ch: 4 (over y).
Axes of the slice: x: 4, y: 4, z: 8, core: 2. Of those that a mesh axis runs over, the one named last changes fastest.
Arguments:
- inputs: bfloat16 [8192, 4096], P('seq'), may hold values from -6 to 6
- norm_gain: float32 [4096], replicated, may hold values from 0.1 to 1.9
- in_weight: bfloat16 [4096, 3, 1024], P('seq', None, 'ch'), may hold values from -0.09375 to 0.09375
- short_filter: float32 [3, 3, 1024], P(None, None, 'ch'), may hold values from -4 to 4
- long_filter: float32 [8192, 1024], P('seq', 'ch'), may hold values from -2.2 to 2.2
- conv_bias: float32 [1024], P('ch'), may hold values from -4 to 4
- out_weight: bfloat16 [1024, 4096], P('ch', 'seq'), may hold values from -0.1875 to 0.1875
- out_grad: bfloat16 [8192, 4096], P('seq'), may hold values from -6 to 6
Outputs:
- block_out: bfloat16 [8192, 4096], P('seq', 'ch')
- in_grad: bfloat16 [8192, 4096], P('seq')
- filter_grad: float32 [8192, 1024], P('seq', 'ch')
All inputs are finite; a program needn't handle non-finite values.
Results may differ from a plain program's by a relative error of at most 0.013.
Values may be sent and summed in bfloat16 or wider, within the bound.
No kernel may reach another device: no remote copies, remote signals or barrier semaphores. Data moves between devices by JAX's collectives and lax.ppermute only.
A program may use at most 64 MiB of HBM per device.

v0:
```python
import math
import jax
import jax.numpy as jnp
from jax import lax
from jax.sharding import PartitionSpec as P

epsilon = 1e-05
highest = lax.Precision.HIGHEST


def passed_along(block, axis, distance):
    devices = range(lax.axis_size(axis))
    route = [(i - distance, i) for i in devices if i - distance in devices]
    return lax.ppermute(block, axis, route)


def to_columns(signals):
    return lax.all_to_all(signals, "seq", split_axis=1, concat_axis=2, tiled=True)


def to_rows(signals):
    return lax.all_to_all(signals, "seq", split_axis=2, concat_axis=1, tiled=True)


def turn_table(rows, cols, period, sign):
    turns = jnp.arange(rows, dtype=jnp.int32)[:, None] * jnp.arange(cols, dtype=jnp.int32)[None, :]
    phases = sign * 2.0 * math.pi / period * (turns % period).astype(jnp.float32)
    return (jnp.cos(phases), jnp.sin(phases))


def fft_sizes(seq_total):
    total = 2 * seq_total
    inner = 1
    while inner * inner < total:
        inner *= 2
    return (total // inner, inner)


def forward_dft(signals):
    count, chans, seq_total = signals.shape
    outer, inner = fft_sizes(seq_total)
    grid = signals.reshape(count, chans, outer // 2, inner)
    cos_out, sin_out = turn_table(outer, outer // 2, outer, 1.0)
    first_real = jnp.einsum("kn,ucnm->uckm", cos_out, grid, precision=highest)
    first_imag = -jnp.einsum("kn,ucnm->uckm", sin_out, grid, precision=highest)
    cos_tw, sin_tw = turn_table(outer, inner, outer * inner, 1.0)
    turned_real = first_real * cos_tw + first_imag * sin_tw
    turned_imag = first_imag * cos_tw - first_real * sin_tw
    cos_in, sin_in = turn_table(inner, inner, inner, 1.0)
    spec_real = jnp.einsum("uckm,mj->uckj", turned_real, cos_in, precision=highest) + jnp.einsum(
        "uckm,mj->uckj", turned_imag, sin_in, precision=highest
    )
    spec_imag = jnp.einsum("uckm,mj->uckj", turned_imag, cos_in, precision=highest) - jnp.einsum(
        "uckm,mj->uckj", turned_real, sin_in, precision=highest
    )
    return (spec_real, spec_imag)


def inverse_dft(spec_real, spec_imag):
    count, chans, outer, inner = spec_real.shape
    cos_in, sin_in = turn_table(inner, inner, inner, 1.0)
    back_real = jnp.einsum("uckj,jm->uckm", spec_real, cos_in, precision=highest) - jnp.einsum(
        "uckj,jm->uckm", spec_imag, sin_in, precision=highest
    )
    back_imag = jnp.einsum("uckj,jm->uckm", spec_imag, cos_in, precision=highest) + jnp.einsum(
        "uckj,jm->uckm", spec_real, sin_in, precision=highest
    )
    cos_tw, sin_tw = turn_table(outer, inner, outer * inner, 1.0)
    turned_real = back_real * cos_tw - back_imag * sin_tw
    turned_imag = back_imag * cos_tw + back_real * sin_tw
    cos_out, sin_out = turn_table(outer, outer // 2, outer, 1.0)
    grid = jnp.einsum("kn,uckm->ucnm", cos_out, turned_real, precision=highest) - jnp.einsum(
        "kn,uckm->ucnm", sin_out, turned_imag, precision=highest
    )
    return grid.reshape(count, chans, outer * inner // 2) / float(outer * inner)


def per_device(
    inputs, norm_gain, in_weight, short_filter, long_filter, conv_bias, out_weight, out_grad
):
    local_rows = inputs.shape[0]
    model_width = inputs.shape[1]
    slab_width = long_filter.shape[1]
    taps = short_filter.shape[1]
    wide_inputs = inputs.astype(jnp.float32)
    inv_rms = lax.rsqrt(jnp.mean(wide_inputs * wide_inputs, axis=1, keepdims=True) + epsilon)
    normed = (wide_inputs * inv_rms * norm_gain).astype(jnp.bfloat16)
    in_panel, out_panel = (
        lax.all_gather(in_weight, "seq", axis=0, tiled=True),
        lax.all_gather(out_weight, "seq", axis=1, tiled=True),
    )
    in_flat = in_panel.reshape(model_width, 3 * slab_width)
    projected = jnp.dot(normed, in_flat, preferred_element_type=jnp.float32)
    projected = projected.astype(jnp.bfloat16).reshape(local_rows, 3, slab_width)
    upper_rim = passed_along(projected[local_rows - (taps - 1) :], "seq", 1)
    extended = jnp.concatenate([upper_rim, projected], 0).astype(jnp.float32)
    mixed = jnp.zeros((local_rows, 3, slab_width), jnp.float32)
    for offset in range(taps):
        begin = taps - 1 - offset
        mixed = mixed + short_filter[:, offset, :][None] * extended[begin : begin + local_rows]
    query_br = mixed[:, 0]
    key_br = mixed[:, 1]
    value_br = mixed[:, 2]
    product = key_br * value_br
    gate_grad = jnp.dot(out_grad, out_panel.T, preferred_element_type=jnp.float32)
    carried = gate_grad * query_br
    columns = to_columns(jnp.stack([product, long_filter, carried]).transpose(0, 2, 1))
    all_real, all_imag = forward_dft(columns)
    sig_real, filt_real, grad_real = (all_real[0], all_real[1], all_real[2])
    sig_imag, filt_imag, grad_imag = (all_imag[0], all_imag[1], all_imag[2])
    conv_real = sig_real * filt_real - sig_imag * filt_imag
    conv_imag = sig_real * filt_imag + sig_imag * filt_real
    back_real = grad_real * filt_real + grad_imag * filt_imag
    back_imag = grad_imag * filt_real - grad_real * filt_imag
    pair_real = grad_real * sig_real + grad_imag * sig_imag
    pair_imag = grad_imag * sig_real - grad_real * sig_imag
    outs = inverse_dft(
        jnp.stack([conv_real, back_real, pair_real]), jnp.stack([conv_imag, back_imag, pair_imag])
    )
    returned = to_rows(outs).transpose(0, 2, 1)
    conv_out = returned[0]
    back_conv = returned[1]
    filter_grad = returned[2] * float(local_rows * lax.axis_size("seq")) ** (-0.5)
    biased = conv_out + conv_bias * product
    gated = (query_br * biased).astype(jnp.bfloat16)
    partial_out = jnp.dot(gated, out_panel, preferred_element_type=jnp.float32)
    summed = lax.psum_scatter(
        partial_out.astype(jnp.bfloat16), "ch", scatter_dimension=1, tiled=True
    ).astype(jnp.float32)
    share = summed.shape[1]
    residual = lax.dynamic_slice_in_dim(wide_inputs, lax.axis_index("ch") * share, share, 1)
    block_out = (residual + summed).astype(jnp.bfloat16)
    source_grad = back_conv + conv_bias * carried
    mixed_grad = jnp.stack([gate_grad * biased, source_grad * value_br, source_grad * key_br], 1)
    lower_rim = passed_along(mixed_grad[: taps - 1], "seq", -1)
    extended_back = jnp.concatenate([mixed_grad, lower_rim], 0)
    proj_grad = jnp.zeros((local_rows, 3, slab_width), jnp.float32)
    for offset in range(taps):
        proj_grad = (
            proj_grad
            + short_filter[:, offset, :][None] * extended_back[offset : offset + local_rows]
        )
    proj_grad = proj_grad.astype(jnp.bfloat16).reshape(local_rows, 3 * slab_width)
    partial_grad = jnp.dot(proj_grad, in_flat.T, preferred_element_type=jnp.float32)
    norm_grad = lax.psum(partial_grad, "ch")
    weighted = norm_grad * norm_gain
    inner_term = jnp.mean(weighted * wide_inputs, axis=1, keepdims=True)
    in_grad = (
        out_grad.astype(jnp.float32) + weighted * inv_rms - wide_inputs * inv_rms**3 * inner_term
    ).astype(jnp.bfloat16)
    return (block_out, in_grad, filter_grad)


def solution(mesh):
    return jax.shard_map(
        per_device,
        mesh=mesh,
        in_specs=(
            P("seq", None),
            P(),
            P("seq", None, "ch"),
            P(None, None, "ch"),
            P("seq", "ch"),
            P("ch"),
            P("ch", "seq"),
            P("seq", None),
        ),
        out_specs=(P("seq", "ch"), P("seq", None), P("seq", "ch")),
        check_vma=False,
    )
```

profile of v0, /device:TPU:1, one launch (start us, length us, event | category | flops | bytes accessed | tf_op | source)
XLA Modules:
  0.0 393.4 jit_solution(6677568835043596494)
XLA Ops:
  11.6 83.9 %all-gather.3.cloned.1.call-done = bf16[4096,3,256]{2,0,1:T(8,128)(2,1)} async-done(((bf16[64,3,256]{2,0,1:T(8,128)(2,1)}), bf16[4096,3,256]{2,0,1:T(8,128)(2,1)}) %all-gather.3.cloned.1.call-update) | async-done | bytes 6291472 | tf_op jit(solution)/shard_map/all_gather | solution.py:89
  95.5 8.7 %copy.46 = bf16[4096,3,256]{0,2,1:T(8,128)(2,1)} copy(bf16[4096,3,256]{2,0,1:T(8,128)(2,1)} %all-gather.3.cloned.1.call-done) | data formatting | bytes 12582912 | tf_op jit(solution)/shard_map/all_gather | solution.py:89
  104.2 5.1 %convolution_convert_fusion.1 = bf16[128,768]{1,0:T(8,128)(2,1)S(1)} fusion(bf16[4096,768]{0,1:T(8,128)(2,1)} %bitcast.127, bf16[128,4096]{1,0:T(8,128)(2,1)S(1)} %copy-done, f32[4096]{0:T(1024)S(1)} %copy-done.9, f32[128]{0:T(128)S(1)} %get-tuple-element.19), kind=kOutput, calls=%fused_computation.16 | convolution fusion | flops 807501824 | bytes 7553536 | tf_op jit(solution)/shard_map/dot_general | solution.py:93
  109.3 2.7 collective-permute-start
  112.1 60.2 %all-gather.5.cloned.1.call-done = bf16[256,4096]{0,1:T(8,128)(2,1)} async-done(((bf16[256,64]{0,1:T(8,128)(2,1)}), bf16[256,4096]{0,1:T(8,128)(2,1)}) %all-gather.5.cloned.1.call-update) | async-done | bytes 2097168 | tf_op jit(solution)/shard_map/all_gather | solution.py:90
  172.3 2.0 fusion.143
  176.4 6.6 %all-to-all-start = ((f32[3,256,128]{2,0,1:T(4,128)}), f32[3,256,128]{2,0,1:T(4,128)S(1)}, u32[]{:S(2)}, u32[]{:S(2)}) async-start(f32[3,256,128]{2,0,1:T(4,128)} %copy.50), calls=%async_computation | async-start | bytes 1048576 | tf_op jit(solution)/shard_map/all_to_all | solution.py:18
  183.9 16.3 %all-to-all-done = f32[3,256,128]{2,0,1:T(4,128)S(1)} async-done(((f32[3,256,128]{2,0,1:T(4,128)}), f32[3,256,128]{2,0,1:T(4,128)S(1)}, u32[]{:S(2)}, u32[]{:S(2)}) %all-to-all-start) | async-done | bytes 393248 | tf_op jit(solution)/shard_map/all_to_all | solution.py:18
  203.3 1.6 fusion.31
  204.9 1.6 fusion.32
  206.5 1.6 convolution_add_fusion.1
  208.1 1.6 convolution_subtract_fusion.1
  217.0 8.6 %copy.85 = f32[3,4,64,128]{1,0,3,2:T(4,128)} copy(f32[3,4,64,128]{3,2,1,0:T(8,128)S(1)} %fusion.2) | data formatting | bytes 786432 | tf_op jit(solution)/shard_map/div | solution.py:75
  225.6 16.0 %reshape.105 = f32[64,1,1536]{2,1,0:T(1,128)S(1)} reshape(f32[8192,3,4]{2,1,0:T(4,128)} %bitcast.125) | data formatting | bytes 786432
  241.6 20.6 %all_to_all.33 = f32[64,1,1536]{2,1,0:T(1,128)S(1)} all-to-all(f32[64,1,1536]{2,1,0:T(1,128)S(1)} %reshape.105), channel_id=1, replica_groups=mesh['seq'=64,'ch'=4] {'seq'}, dimensions={0} | all-to-all | bytes 786432 | tf_op jit(solution)/shard_map/all_to_all | solution.py:22
  262.8 1.6 reduce
  264.4 11.6 %reshape.106 = f32[8192,3,4]{2,1,0:T(4,128)} reshape(f32[64,1536]{1,0:T(8,128)S(1)} %reduce) | data formatting | bytes 786432
  275.9 10.1 %copy.86 = f32[3,4,64,128]{3,2,1,0:T(8,128)} copy(f32[3,4,64,128]{1,0,3,2:T(4,128)} %bitcast.126) | data formatting | bytes 786432 | tf_op jit(solution)/shard_map/all_to_all | solution.py:22
  286.0 2.2 copy.67
  288.1 1.9 copy.68
  290.0 1.8 fusion.37
  291.9 1.8 convolution_convert_fusion
  295.7 2.6 collective-permute-start.1
  298.3 2.4 collective-permute-done.1
  300.7 6.4 %convolution_bitcast_fusion = f32[128,4096]{1,0:T(8,128)} fusion(bf16[4096,3,256]{2,0,1:T(8,128)(2,1)} %all-gather.3.cloned.1.call-done, f32[130,3,256]{2,0,1:T(8,128)S(1)} %pad_maximum_fusion.6, f32[3,256]{1,0:T(4,128)S(1)} %get-tuple-element.20, f32[3,256]{1,0:T(4,128)S(1)} %get-tuple-element.21, f32[3,256]{1,0:T(4,128)S(1)} %bitcast.136, ...), kind=kOutput, calls=%fused_computation | convolution fusion | flops 806092800 | bytes 9580544 | tf_op jit(solution)/shard_map/dot_general | solution.py:144
  307.2 1.6 convert_element_type.86
  308.7 1.6 fusion.33
  310.3 5.3 %reduce-scatter.2.cloned.1.call-done = bf16[128,1024]{1,0:T(8,128)(2,1)} async-done(((bf16[128,4096]{1,0:T(8,128)(2,1)}), bf16[128,1024]{1,0:T(8,128)(2,1)}) %reduce-scatter.2.cloned.1.call-update) | async-done | bytes 262160 | tf_op jit(solution)/shard_map/reduce_scatter | solution.py:127
  315.6 1.9 add_convert_fusion
  317.5 65.3 %all-reduce.2.cloned.1.call-done = f32[128,4096]{1,0:T(8,128)} async-done(((f32[128,4096]{1,0:T(8,128)}), f32[128,4096]{1,0:T(8,128)}) %all-reduce.2.cloned.1.call-update) | async-done | bytes 2097168 | tf_op jit(solution)/shard_map/psum | solution.py:145
  382.8 2.1 multiply_reduce_fusion
  385.0 1.9 subtract_convert_fusion
  (73 shorter events, 20.2 us)
Async XLA Ops:
  7.2 88.3 %all-gather.3.cloned.1.call-start = ((), (), s32[]{:S(2)}) async-start(), calls=%async_computation.3 | async-start | bytes 6389760 | tf_op jit(solution)/shard_map/all_gather | solution.py:89
  7.9 164.4 %all-gather.5.cloned.1.call-start = ((), (), s32[]{:S(2)}) async-start(), calls=%async_computation.4 | async-start | bytes 2129920 | tf_op jit(solution)/shard_map/all_gather | solution.py:90
  11.6 92.6 %copy-start.13 = (f32[128]{0:T(128)}, f32[128]{0:T(128)S(1)}, u32[]{:S(2)}) copy-start(f32[128]{0:T(128)S(1)} %get-tuple-element.19) | copy-start | bytes 1540
  11.6 92.6 %copy-start = (bf16[128,4096]{1,0:T(8,128)(2,1)S(1)}, bf16[128,4096]{1,0:T(8,128)(2,1)}, u32[]{:S(2)}) copy-start(bf16[128,4096]{1,0:T(8,128)(2,1)} %param.8) | copy-start | bytes 3145732
  11.6 92.6 %copy-start.9 = (f32[4096]{0:T(1024)S(1)}, f32[4096]{0:T(1024)}, u32[]{:S(2)}) copy-start(f32[4096]{0:T(1024)} %param.9) | copy-start | bytes 49156
  104.2 68.1 %copy-start.3 = (bf16[128,4096]{1,0:T(8,128)(2,1)S(1)}, bf16[128,4096]{1,0:T(8,128)(2,1)}, u32[]{:S(2)}) copy-start(bf16[128,4096]{1,0:T(8,128)(2,1)} %param.15) | copy-start | bytes 3145732
  109.3 65.4 %collective-permute-start = (bf16[2,3,256]{2,0,1:T(2,128)(2,1)S(1)}, bf16[2,3,256]{2,0,1:T(2,128)(2,1)S(1)}, u32[]{:S(2)}, u32[]{:S(2)}) collective-permute-start(bf16[2,3,256]{2,0,1:T(2,128)(2,1)S(1)} %bitcast.138), channel_id=1, source_target_pairs={{0,4},{4,8},{8,12},{12,16},{16,20},{20,24},{24,28},{28,32},{32,36}... | collective-permute-start | bytes 9224 | tf_op jit(solution)/shard_map/ppermute | solution.py:14
  174.4 1.0 copy-start.7
  174.4 1.0 copy-start.8
  176.4 23.9 %all-to-all-start = ((f32[3,256,128]{2,0,1:T(4,128)}), f32[3,256,128]{2,0,1:T(4,128)S(1)}, u32[]{:S(2)}, u32[]{:S(2)}) async-start(f32[3,256,128]{2,0,1:T(4,128)} %copy.50), calls=%async_computation | async-start | bytes 1048576 | tf_op jit(solution)/shard_map/all_to_all | solution.py:18
  183.0 132.6 %reduce-scatter.2.cloned.1.call-start = ((), (), s32[]{:S(2)}) async-start(), calls=%async_computation.5 | async-start | bytes 1310720 | tf_op jit(solution)/shard_map/reduce_scatter | solution.py:127
  275.9 14.1 %copy-start.11 = (f32[256]{0:T(256)S(1)}, f32[256]{0:T(256)}, u32[]{:S(2)}) copy-start(f32[256]{0:T(256)} %param.13) | copy-start | bytes 3076
  286.0 5.9 %copy-start.1 = (bf16[256,4096]{0,1:T(8,128)(2,1)S(1)}, bf16[256,4096]{0,1:T(8,128)(2,1)}, u32[]{:S(2)}) copy-start(bf16[256,4096]{0,1:T(8,128)(2,1)} %all-gather.5.cloned.1.call-done) | copy-start | bytes 6291460
  293.6 7.0 %copy-start.5 = (f32[128,1,256]{2,0,1:T(8,128)S(1)}, f32[128,1,256]{2,0,1:T(8,128)}, u32[]{:S(2)}) copy-start(f32[128,1,256]{2,0,1:T(8,128)} %get-tuple-element.5) | copy-start | bytes 393220
  293.6 7.0 %copy-start.6 = (f32[128,1,256]{2,0,1:T(8,128)S(1)}, f32[128,1,256]{2,0,1:T(8,128)}, u32[]{:S(2)}) copy-start(f32[128,1,256]{2,0,1:T(8,128)} %get-tuple-element.13) | copy-start | bytes 393220
  293.7 89.1 %all-reduce.2.cloned.1.call-start = ((), (), s32[]{:S(2)}) async-start(), calls=%async_computation.6 | async-start | bytes 4194304 | tf_op jit(solution)/shard_map/psum | solution.py:145
  295.7 4.9 %collective-permute-start.1 = (f32[2,3,256]{2,0,1:T(2,128)S(1)}, f32[2,3,256]{2,0,1:T(2,128)S(1)}, u32[]{:S(2)}, u32[]{:S(2)}) collective-permute-start(f32[2,3,256]{2,0,1:T(2,128)S(1)} %slice.110), channel_id=1, source_target_pairs={{4,0},{8,4},{12,8},{16,12},{20,16},{24,20},{28,24},{32,28},{36,32}... | collective-permute-start | bytes 18440 | tf_op jit(solution)/shard_map/ppermute | solution.py:14
  307.1 75.6 %copy-start.10 = (f32[4096]{0:T(1024)S(1)}, f32[4096]{0:T(1024)}, u32[]{:S(2)}) copy-start(f32[4096]{0:T(1024)} %param.9) | copy-start | bytes 49156
  310.3 74.6 %copy-start.4 = (bf16[128,4096]{1,0:T(8,128)(2,1)S(1)}, bf16[128,4096]{1,0:T(8,128)(2,1)}, u32[]{:S(2)}) copy-start(bf16[128,4096]{1,0:T(8,128)(2,1)} %param.15) | copy-start | bytes 3145732
  310.3 74.6 %copy-start.12 = (f32[128]{0:T(128)S(1)}, f32[128]{0:T(128)}, u32[]{:S(2)}) copy-start(f32[128]{0:T(128)} %get-tuple-element.18) | copy-start | bytes 1540
  310.3 74.6 %copy-start.14 = (f32[128]{0:T(128)S(1)}, f32[128]{0:T(128)}, u32[]{:S(2)}) copy-start(f32[128]{0:T(128)} %copy-done.13) | copy-start | bytes 1540
  382.8 2.2 copy-start.2
Sparse Core Ops, SparseCore 0:
  10.8 84.6 all-gather.2
  98.3 74.0 all-gather.4
  293.8 21.7 reduce-scatter.1
  317.8 64.9 all-reduce.1
where the time goes:
time: 395 us; the launch traced here: 393 us
  waiting for transfers between devices  235 us (59%)
  local copies, waits for them, and re-layouts  62.4 us (16%)
  matrix products  31.7 us (8%)
  blocking collectives  20.6 us (5%)
  other arithmetic  17.5 us (4%)
  between operations  14.1 us (4%)
  starting transfers between devices  12.2 us (3%)
    all_gather x1, waiting for transfers between devices, per_device(): lax.all_gather(in_weight, 'seq', axis=0, tiled=True)  83.9 us
    psum x1, waiting for transfers between devices, per_device(): norm_grad = lax.psum(partial_grad, 'ch')  65.3 us
    all_gather x1, waiting for transfers between devices, per_device(): lax.all_gather(out_weight, 'seq', axis=1, tiled=True)  60.2 us
    unnamed x34, local copies, waits for them, and re-layouts  28.1 us
    all_to_all x1, blocking collectives, to_rows(): lax.all_to_all(signals, 'seq', split_axis=2, concat_axis=1, tiled=True)  20.6 us
    all_to_all x1, waiting for transfers between devices, to_columns(): lax.all_to_all(signals, 'seq', split_axis=1, concat_axis=2, tiled=True)  16.3 us
    all_to_all x4, local copies, waits for them, and re-layouts, to_rows(): lax.all_to_all(signals, 'seq', split_axis=2, concat_axis=1, tiled=True)  14.6 us
    all_gather x1, local copies, waits for them, and re-layouts, per_device(): lax.all_gather(in_weight, 'seq', axis=0, tiled=True)  8.7 us
  transfers between devices with their start and end apart: 7, of which 6 were waited for; matrix products, arithmetic and copies ran while one was open for 8% of the time, Pallas kernels for 0%

commit v1 on v0

--- a/solution.py
+++ b/solution.py
@@ -6,6 +6,14 @@
 
 epsilon = 1e-05
 highest = lax.Precision.HIGHEST
+
+
+def added_up(x, name):
+    size, total = (lax.axis_size(name), x)
+    for stride in [1 << k for k in range(size.bit_length() - 1)]:
+        swap = [(i, i ^ stride) for i in range(size)]
+        total = total + lax.ppermute(total, name, swap)
+    return total
 
 
 def passed_along(block, axis, distance):
@@ -142,7 +150,7 @@
         )
     proj_grad = proj_grad.astype(jnp.bfloat16).reshape(local_rows, 3 * slab_width)
     partial_grad = jnp.dot(proj_grad, in_flat.T, preferred_element_type=jnp.float32)
-    norm_grad = lax.psum(partial_grad, "ch")
+    norm_grad = added_up(partial_grad, "ch")
     weighted = norm_grad * norm_gain
     inner_term = jnp.mean(weighted * wide_inputs, axis=1, keepdims=True)
     in_grad = (

time: 395 us -> 416 us (1.053)
  waiting for transfers between devices: 235 us -> 258 us
  local copies, waits for them, and re-layouts: 62.4 us -> 58 us
    ppermute x0 -> x2, waiting for transfers between devices: none -> 93.3 us  [added_up(): total = total + lax.ppermute(total, name, swap)]
    psum x1 -> x0, waiting for transfers between devices: 65.3 us -> none  [per_device(): norm_grad = lax.psum(partial_grad, 'ch')]
    reduce_scatter x1, waiting for transfers between devices: 5.28 us -> 0.01 us  [per_device(): lax.psum_scatter(partial_out.astype(jnp.bfloat16), 'ch', scatter_dimensio...]
    all_to_all x4, local copies, waits for them, and re-layouts: 14.6 us -> 10.3 us  [to_rows(): lax.all_to_all(signals, 'seq', split_axis=2, concat_axis=1, tiled=True)]
    unnamed x34 -> x28, local copies, waits for them, and re-layouts: 28.1 us -> 28 us
  transfers between devices with their start and end apart: 7 -> 8, of which waited for: 6 -> 6; matrix products, arithmetic and copies ran while one was open for 8% -> 7% of each run, Pallas kernels for 0% -> 0%
where the time goes in v1:
time: 416 us; the launch traced here: 415 us
  waiting for transfers between devices  258 us (62%)
  local copies, waits for them, and re-layouts  58 us (14%)
  matrix products  30.4 us (7%)
  blocking collectives  20.6 us (5%)
  other arithmetic  17.1 us (4%)
  starting transfers between devices  16.1 us (4%)
  between operations  14.2 us (3%)
    ppermute x2, waiting for transfers between devices, added_up(): total = total + lax.ppermute(total, name, swap)  93.3 us
    all_gather x1, waiting for transfers between devices, per_device(): lax.all_gather(in_weight, 'seq', axis=0, tiled=True)  84.4 us
    all_gather x1, waiting for transfers between devices, per_device(): lax.all_gather(out_weight, 'seq', axis=1, tiled=True)  60.2 us
    unnamed x28, local copies, waits for them, and re-layouts  28 us
    all_to_all x1, blocking collectives, to_rows(): lax.all_to_all(signals, 'seq', split_axis=2, concat_axis=1, tiled=True)  20.6 us
    all_to_all x1, waiting for transfers between devices, to_columns(): lax.all_to_all(signals, 'seq', split_axis=1, concat_axis=2, tiled=True)  16.3 us
    all_to_all x4, local copies, waits for them, and re-layouts, to_rows(): lax.all_to_all(signals, 'seq', split_axis=2, concat_axis=1, tiled=True)  10.3 us
    all_gather x1, local copies, waits for them, and re-layouts, per_device(): lax.all_gather(in_weight, 'seq', axis=0, tiled=True)  8.71 us
  transfers between devices with their start and end apart: 8, of which 6 were waited for; matrix products, arithmetic and copies ran while one was open for 7% of the time, Pallas kernels for 0%

profile of v1, /device:TPU:1, one launch (start us, length us, event | category | flops | bytes accessed | tf_op | source)
XLA Modules:
  0.0 414.7 jit_solution(11541212020376695205)
XLA Ops:
  9.5 1.5 multiply_reduce_fusion.1
  11.1 84.4 %all-gather.3.cloned.1.call-done = bf16[4096,3,256]{2,0,1:T(8,128)(2,1)} async-done(((bf16[64,3,256]{2,0,1:T(8,128)(2,1)}), bf16[4096,3,256]{2,0,1:T(8,128)(2,1)}) %all-gather.3.cloned.1.call-update) | async-done | bytes 6291472 | tf_op jit(solution)/shard_map/all_gather | solution.py:97
  95.5 8.7 %copy.46 = bf16[4096,3,256]{0,2,1:T(8,128)(2,1)} copy(bf16[4096,3,256]{2,0,1:T(8,128)(2,1)} %all-gather.3.cloned.1.call-done) | data formatting | bytes 12582912 | tf_op jit(solution)/shard_map/all_gather | solution.py:97
  104.2 5.1 %convolution_convert_fusion.1 = bf16[128,768]{1,0:T(8,128)(2,1)S(1)} fusion(bf16[4096,768]{0,1:T(8,128)(2,1)} %bitcast.127, bf16[128,4096]{1,0:T(8,128)(2,1)S(1)} %copy-done, f32[4096]{0:T(1024)S(1)} %copy-done.7, f32[128]{0:T(128)S(1)} %get-tuple-element.19), kind=kOutput, calls=%fused_computation.17 | convolution fusion | flops 807501824 | bytes 7553536 | tf_op jit(solution)/shard_map/dot_general | solution.py:101
  109.4 2.7 collective-permute-start
  112.1 60.2 %all-gather.5.cloned.1.call-done = bf16[256,4096]{0,1:T(8,128)(2,1)} async-done(((bf16[256,64]{0,1:T(8,128)(2,1)}), bf16[256,4096]{0,1:T(8,128)(2,1)}) %all-gather.5.cloned.1.call-update) | async-done | bytes 2097168 | tf_op jit(solution)/shard_map/all_gather | solution.py:98
  172.3 2.0 fusion.143
  176.3 6.6 %all-to-all-start = ((f32[3,256,128]{2,0,1:T(4,128)}), f32[3,256,128]{2,0,1:T(4,128)S(1)}, u32[]{:S(2)}, u32[]{:S(2)}) async-start(f32[3,256,128]{2,0,1:T(4,128)} %copy.50), calls=%async_computation | async-start | bytes 1048576 | tf_op jit(solution)/shard_map/all_to_all | solution.py:26
  183.9 16.3 %all-to-all-done = f32[3,256,128]{2,0,1:T(4,128)S(1)} async-done(((f32[3,256,128]{2,0,1:T(4,128)}), f32[3,256,128]{2,0,1:T(4,128)S(1)}, u32[]{:S(2)}, u32[]{:S(2)}) %all-to-all-start) | async-done | bytes 393248 | tf_op jit(solution)/shard_map/all_to_all | solution.py:26
  203.2 1.6 fusion.31
  204.8 1.6 fusion.32
  206.4 1.6 convolution_add_fusion.1
  208.0 1.6 convolution_subtract_fusion.1
  216.9 8.7 %copy.85 = f32[3,4,64,128]{1,0,3,2:T(4,128)} copy(f32[3,4,64,128]{3,2,1,0:T(8,128)S(1)} %fusion.2) | data formatting | bytes 786432 | tf_op jit(solution)/shard_map/div | solution.py:83
  225.5 16.0 %reshape.105 = f32[64,1,1536]{2,1,0:T(1,128)S(1)} reshape(f32[8192,3,4]{2,1,0:T(4,128)} %bitcast.125) | data formatting | bytes 786432
  241.6 20.6 %all_to_all.33 = f32[64,1,1536]{2,1,0:T(1,128)S(1)} all-to-all(f32[64,1,1536]{2,1,0:T(1,128)S(1)} %reshape.105), channel_id=1, replica_groups=mesh['seq'=64,'ch'=4] {'seq'}, dimensions={0} | all-to-all | bytes 786432 | tf_op jit(solution)/shard_map/all_to_all | solution.py:30
  262.7 1.6 reduce
  264.3 11.6 %reshape.106 = f32[8192,3,4]{2,1,0:T(4,128)} reshape(f32[64,1536]{1,0:T(8,128)S(1)} %reduce) | data formatting | bytes 786432
  275.9 9.4 %copy.86 = f32[3,4,64,128]{3,2,1,0:T(8,128)S(1)} copy(f32[3,4,64,128]{1,0,3,2:T(4,128)} %bitcast.126) | data formatting | bytes 786432 | tf_op jit(solution)/shard_map/all_to_all | solution.py:30
  285.9 2.3 collective-permute-start.1
  288.2 2.6 collective-permute-done.1
  290.9 5.1 %convolution_bitcast_fusion = f32[128,4096]{1,0:T(8,128)S(1)} fusion(bf16[4096,3,256]{2,0,1:T(8,128)(2,1)} %all-gather.3.cloned.1.call-done, f32[130,3,256]{2,0,1:T(8,128)S(1)} %pad_maximum_fusion.6, f32[3,256]{1,0:T(4,128)S(1)} %get-tuple-element.20, f32[3,256]{1,0:T(4,128)S(1)} %get-tuple-element.21, f32[3,256]{1,0:T(4,128)S(1)} %bitcast.136, ...), kind=kOutput, calls=%fused_computation | convolution fusion | flops 806092800 | bytes 9580544 | tf_op jit(solution)/shard_map/dot_general | solution.py:152
  297.3 1.8 convolution_convert_fusion
  299.1 51.8 %collective-permute-done.2 = f32[128,4096]{1,0:T(8,128)} collective-permute-done((f32[128,4096]{1,0:T(8,128)S(1)}, f32[128,4096]{1,0:T(8,128)}, u32[]{:S(2)}, u32[]{:S(2)}) %collective-permute-start.2) | collective-permute-done | bytes 2097184 | tf_op jit(solution)/shard_map/ppermute | solution.py:15
  350.9 2.4 add.156
  353.4 2.8 collective-permute-start.3
  356.2 1.5 convert_element_type.86
  357.7 1.6 fusion.33
  359.3 1.9 add_convert_fusion
  361.2 41.4 %collective-permute-done.3 = f32[128,4096]{1,0:T(8,128)} collective-permute-done((f32[128,4096]{1,0:T(8,128)S(1)}, f32[128,4096]{1,0:T(8,128)}, u32[]{:S(2)}, u32[]{:S(2)}) %collective-permute-start.3) | collective-permute-done | bytes 2097184 | tf_op jit(solution)/shard_map/ppermute | solution.py:15
  402.6 2.0 multiply_reduce_fusion
  404.6 3.5 subtract_convert_fusion
  (69 shorter events, 17.7 us)
Async XLA Ops:
  7.2 88.3 %all-gather.3.cloned.1.call-start = ((), (), s32[]{:S(2)}) async-start(), calls=%async_computation.3 | async-start | bytes 6389760 | tf_op jit(solution)/shard_map/all_gather | solution.py:97
  7.9 164.4 %all-gather.5.cloned.1.call-start = ((), (), s32[]{:S(2)}) async-start(), calls=%async_computation.4 | async-start | bytes 2129920 | tf_op jit(solution)/shard_map/all_gather | solution.py:98
  11.0 93.2 %copy-start.10 = (f32[128]{0:T(128)}, f32[128]{0:T(128)S(1)}, u32[]{:S(2)}) copy-start(f32[128]{0:T(128)S(1)} %get-tuple-element.19) | copy-start | bytes 1540
  11.0 93.2 %copy-start = (bf16[128,4096]{1,0:T(8,128)(2,1)S(1)}, bf16[128,4096]{1,0:T(8,128)(2,1)}, u32[]{:S(2)}) copy-start(bf16[128,4096]{1,0:T(8,128)(2,1)} %param.8) | copy-start | bytes 3145732
  11.1 93.2 %copy-start.7 = (f32[4096]{0:T(1024)S(1)}, f32[4096]{0:T(1024)}, u32[]{:S(2)}) copy-start(f32[4096]{0:T(1024)} %param.9) | copy-start | bytes 49156
  104.2 68.1 %copy-start.3 = (bf16[128,4096]{1,0:T(8,128)(2,1)S(1)}, bf16[128,4096]{1,0:T(8,128)(2,1)}, u32[]{:S(2)}) copy-start(bf16[128,4096]{1,0:T(8,128)(2,1)} %param.15) | copy-start | bytes 3145732
  109.4 65.4 %collective-permute-start = (bf16[2,3,256]{2,0,1:T(2,128)(2,1)S(1)}, bf16[2,3,256]{2,0,1:T(2,128)(2,1)S(1)}, u32[]{:S(2)}, u32[]{:S(2)}) collective-permute-start(bf16[2,3,256]{2,0,1:T(2,128)(2,1)S(1)} %bitcast.138), channel_id=1, source_target_pairs={{0,4},{4,8},{8,12},{12,16},{16,20},{20,24},{24,28},{28,32},{32,36}... | collective-permute-start | bytes 9224 | tf_op jit(solution)/shard_map/ppermute | solution.py:22
  174.4 0.9 copy-start.6
  176.3 23.9 %all-to-all-start = ((f32[3,256,128]{2,0,1:T(4,128)}), f32[3,256,128]{2,0,1:T(4,128)S(1)}, u32[]{:S(2)}, u32[]{:S(2)}) async-start(f32[3,256,128]{2,0,1:T(4,128)} %copy.50), calls=%async_computation | async-start | bytes 1048576 | tf_op jit(solution)/shard_map/all_to_all | solution.py:26
  182.9 176.3 %reduce-scatter.2.cloned.1.call-start = ((), (), s32[]{:S(2)}) async-start(), calls=%async_computation.5 | async-start | bytes 1310720 | tf_op jit(solution)/shard_map/reduce_scatter | solution.py:135
  275.9 9.8 %copy-start.9 = (f32[256]{0:T(256)S(1)}, f32[256]{0:T(256)}, u32[]{:S(2)}) copy-start(f32[256]{0:T(256)} %param.13) | copy-start | bytes 3076
  285.7 5.1 %copy-start.5 = (f32[3,256,128]{1,2,0:T(8,128)}, f32[3,256,128]{1,2,0:T(8,128)S(1)}, u32[]{:S(2)}) copy-start(f32[3,256,128]{1,2,0:T(8,128)S(1)} %copy.68) | copy-start | bytes 1179652
  285.9 4.9 %collective-permute-start.1 = (f32[2,3,256]{2,0,1:T(2,128)S(1)}, f32[2,3,256]{2,0,1:T(2,128)S(1)}, u32[]{:S(2)}, u32[]{:S(2)}) collective-permute-start(f32[2,3,256]{2,0,1:T(2,128)S(1)} %slice.110), channel_id=1, source_target_pairs={{4,0},{8,4},{12,8},{16,12},{20,16},{24,20},{28,24},{32,28},{36,32}... | collective-permute-start | bytes 18440 | tf_op jit(solution)/shard_map/ppermute | solution.py:22
  290.8 6.4 %copy-start.1 = (bf16[256,4096]{0,1:T(8,128)(2,1)S(1)}, bf16[256,4096]{0,1:T(8,128)(2,1)}, u32[]{:S(2)}) copy-start(bf16[256,4096]{0,1:T(8,128)(2,1)} %all-gather.5.cloned.1.call-done) | copy-start | bytes 6291460
  296.0 3.1 copy-start.2
  296.0 54.9 %collective-permute-start.2 = (f32[128,4096]{1,0:T(8,128)S(1)}, f32[128,4096]{1,0:T(8,128)}, u32[]{:S(2)}, u32[]{:S(2)}) collective-permute-start(f32[128,4096]{1,0:T(8,128)S(1)} %convolution_bitcast_fusion), channel_id=1, source_target_pairs={{0,1},{1,0},{2,3},{3,2},{4,5},{5,4},{6,7},{7,6},{8,9},{9,8},{10,11... | collective-permute-start | bytes 6291464 | tf_op jit(solution)/shard_map/ppermute | solution.py:15
  353.4 49.2 %collective-permute-start.3 = (f32[128,4096]{1,0:T(8,128)S(1)}, f32[128,4096]{1,0:T(8,128)}, u32[]{:S(2)}, u32[]{:S(2)}) collective-permute-start(f32[128,4096]{1,0:T(8,128)S(1)} %add.156), channel_id=1, source_target_pairs={{0,2},{1,3},{2,0},{3,1},{4,6},{5,7},{6,4},{7,5},{8,10},{9,11},{10,... | collective-permute-start | bytes 6291464 | tf_op jit(solution)/shard_map/ppermute | solution.py:15
  356.2 46.4 %copy-start.8 = (f32[4096]{0:T(1024)S(1)}, f32[4096]{0:T(1024)}, u32[]{:S(2)}) copy-start(f32[4096]{0:T(1024)} %param.9) | copy-start | bytes 49156
  361.2 43.5 %copy-start.4 = (bf16[128,4096]{1,0:T(8,128)(2,1)S(1)}, bf16[128,4096]{1,0:T(8,128)(2,1)}, u32[]{:S(2)}) copy-start(bf16[128,4096]{1,0:T(8,128)(2,1)} %param.15) | copy-start | bytes 3145732
  361.2 43.5 %copy-start.11 = (f32[128]{0:T(128)S(1)}, f32[128]{0:T(128)}, u32[]{:S(2)}) copy-start(f32[128]{0:T(128)} %copy-done.10) | copy-start | bytes 1540
Sparse Core Ops, SparseCore 0:
  10.8 84.6 all-gather.2
  98.3 74.0 all-gather.4
  299.2 28.2 reduce-scatter.1
